TPU v7x, 32 devices: a whole 2x2x4 slice. The times are simulated.
32 devices in a mesh: groups: 2 (over y), seq: 4 (over z), dp: 2 (over x), head: 2 (over core).
Axes of the slice: x: 2, y: 2, z: 4, core: 2. Of those that a mesh axis runs over, the one named last changes fastest.
Arguments:
- queries: bfloat16 [4, 512, 2048], P(('groups', 'dp'), 'seq', 'head'), parts along dimension 0, may hold values from -8 to 8
- keys: bfloat16 [4, 512, 2048], P(('groups', 'dp'), 'seq', 'head'), parts along dimension 0, may hold values from -8 to 8
- values: bfloat16 [4, 512, 2048], P(('groups', 'dp'), 'seq', 'head'), parts along dimension 0, may hold values from -12 to 12
- pattern: int32 [4, 8, 2], P(('groups', 'dp'), 'seq'), parts along dimension 0, may hold values from -2 to 2, as said below
- out_weight: bfloat16 [4096, 2048], P('seq', 'head'), may hold values from -0.125 to 0.125
- cotangent: bfloat16 [4, 512, 4096], P(('groups', 'dp'), 'seq'), parts along dimension 0, may hold values from -6 to 6
Outputs:
- attention: bfloat16 [4, 512, 2048], P(('groups', 'dp'), 'seq', 'head'), parts along dimension 0
- query_grad: bfloat16 [4, 512, 2048], P(('groups', 'dp'), 'seq', 'head'), parts along dimension 0
- key_grad: bfloat16 [4, 512, 2048], P(('groups', 'dp'), 'seq', 'head'), parts along dimension 0
- value_grad: bfloat16 [4, 512, 2048], P(('groups', 'dp'), 'seq', 'head'), parts along dimension 0
- weight_grad: float32 [8192, 2048], P(('groups', 'seq'), 'head'), parts along dimension 0
There are 2 independent parts, one for each index of `groups`. A program takes and returns all parts, laid end to end along the dimension named above; an argument that names none is the same for every part. Nothing has to cross between parts.
Inputs may be any that keep to these rules, and one draw needn't show every extreme that they name: `pattern`: each row holds 2 different block offsets from -2, -1, 1, 2, each keeping the block inside its document.
All inputs are finite; a program needn't handle non-finite values.
Results may differ from a plain program's by a relative error of at most 0.0099.
Values may be sent and summed in bfloat16 or wider, within the bound.
No kernel may reach another device: no remote copies, remote signals or barrier semaphores. Data moves between devices by JAX's collectives and lax.ppermute only.
A program may use at most 128 MiB of HBM per device.

v0:
```python
import math
import jax
import jax.numpy as jnp
from jax import lax
from jax.sharding import PartitionSpec as P

HEAD_DIM = 128
NEAR = 2


def extended(cells, sides, width):
    for axis, dim in sides:
        count = lax.axis_size(axis)
        ends = count - 1
        head = lax.slice_in_dim(cells, 0, width, axis=dim)
        tail = lax.slice_in_dim(cells, cells.shape[dim] - width, cells.shape[dim], axis=dim)
        cells = jnp.concatenate(
            [
                lax.ppermute(tail, axis, [(i, (i + 1) % count) for i in range(ends)]),
                cells,
                lax.ppermute(head, axis, [((i + 1) % count, i) for i in range(ends)]),
            ],
            axis=dim,
        )
    return cells


def swapped(shard, axis, stride):
    return lax.ppermute(shard, axis, [(i, i ^ 1 << stride) for i in range(lax.axis_size(axis))])


def pool_pairs(source):
    shaped = source.reshape(
        source.shape[0], source.shape[1], source.shape[2] // 2, 2, source.shape[3]
    )
    return jnp.sum(shaped, axis=3) * 0.5


def pick_blocks(blocks_doc, chosen_doc):
    return blocks_doc[:, chosen_doc]


def place_blocks(grad_doc, chosen_doc):
    holder = jnp.zeros((grad_doc.shape[0], 6, grad_doc.shape[3], grad_doc.shape[4]), jnp.float32)
    return holder.at[:, chosen_doc].add(grad_doc)


def shards(queries, keys, values, pattern, out_weight, cotangent):
    doc_count, tok_count, head_cols = queries.shape
    block = tok_count // 2
    heads = head_cols // HEAD_DIM
    seq_count = lax.axis_size("seq")
    levels = seq_count.bit_length() - 1
    position = lax.axis_index("seq")
    score_scale = 1.0 / math.sqrt(HEAD_DIM)
    near_width = (NEAR + 1) * block
    key_value = jnp.stack([keys, values])
    padded = extended(key_value, (("seq", 2),), tok_count)
    blocks_six = padded.reshape(2, doc_count, 6, block, head_cols)
    local_ids = jnp.arange(2, dtype=jnp.int32)[None, :, None]
    chosen = jnp.concatenate([local_ids, local_ids + pattern], axis=2) + 2
    near_pair = jax.vmap(pick_blocks, in_axes=(1, 0), out_axes=1)(blocks_six, chosen)
    near_pair = near_pair.reshape(2, doc_count, 2, near_width, head_cols)
    pooled = pool_pairs(key_value.astype(jnp.float32))
    siblings = []
    own_level = pooled
    for level_no in range(levels):
        other = swapped(own_level, "seq", level_no)
        siblings.append(other)
        if level_no + 1 < levels:
            upper = position >> level_no & 1 == 1
            joined = jnp.where(
                upper,
                jnp.concatenate([other, own_level], axis=2),
                jnp.concatenate([own_level, other], axis=2),
            )
            own_level = pool_pairs(joined)
    far_pair = jnp.concatenate(siblings, axis=2).astype(jnp.bfloat16)
    query_heads = queries.reshape(doc_count, 2, block, heads, HEAD_DIM)
    near_k = near_pair[0].reshape(doc_count, 2, near_width, heads, HEAD_DIM)
    near_v = near_pair[1].reshape(doc_count, 2, near_width, heads, HEAD_DIM)
    far_k = far_pair[0].reshape(doc_count, levels * block, heads, HEAD_DIM)
    far_v = far_pair[1].reshape(doc_count, levels * block, heads, HEAD_DIM)
    score_near = (
        jnp.einsum("dbqhe,dbkhe->dbhqk", query_heads, near_k, preferred_element_type=jnp.float32)
        * score_scale
    )
    score_far = (
        jnp.einsum("dbqhe,dkhe->dbhqk", query_heads, far_k, preferred_element_type=jnp.float32)
        * score_scale
    )
    top = jnp.maximum(
        jnp.max(score_near, axis=-1, keepdims=True), jnp.max(score_far, axis=-1, keepdims=True)
    )
    exp_near = jnp.exp(score_near - top)
    exp_far = jnp.exp(score_far - top)
    total = jnp.sum(exp_near, axis=-1, keepdims=True) + jnp.sum(exp_far, axis=-1, keepdims=True)
    weight_near = exp_near / total
    weight_far = exp_far / total
    rounded_near = weight_near.astype(jnp.bfloat16)
    rounded_far = weight_far.astype(jnp.bfloat16)
    output = jnp.einsum(
        "dbhqk,dbkhe->dbqhe", rounded_near, near_v, preferred_element_type=jnp.float32
    )
    output = output + jnp.einsum(
        "dbhqk,dkhe->dbqhe", rounded_far, far_v, preferred_element_type=jnp.float32
    )
    attention = output.reshape(doc_count, tok_count, head_cols).astype(jnp.bfloat16)
    cot_rows = cotangent.reshape(doc_count * tok_count, cotangent.shape[2])
    whole_weight = lax.all_gather(out_weight, "seq", axis=0, tiled=True)
    attn_grad = jnp.dot(cot_rows, whole_weight, preferred_element_type=jnp.float32).astype(
        jnp.bfloat16
    )
    by_feature = lax.all_to_all(cotangent, "seq", split_axis=2, concat_axis=1, tiled=True)
    whole_output = lax.all_gather(attention, "seq", axis=1, tiled=True)
    weight_part = jnp.einsum(
        "dtc,dtw->cw", by_feature, whole_output, preferred_element_type=jnp.float32
    )
    weight_grad = lax.psum(weight_part, "dp")
    grad_heads = attn_grad.reshape(doc_count, 2, block, heads, HEAD_DIM)
    prob_near = jnp.einsum(
        "dbqhe,dbkhe->dbhqk", grad_heads, near_v, preferred_element_type=jnp.float32
    )
    prob_far = jnp.einsum(
        "dbqhe,dkhe->dbhqk", grad_heads, far_v, preferred_element_type=jnp.float32
    )
    row_dot = jnp.sum(weight_near * prob_near, axis=-1, keepdims=True) + jnp.sum(
        weight_far * prob_far, axis=-1, keepdims=True
    )
    grad_near = (weight_near * (prob_near - row_dot)).astype(jnp.bfloat16)
    grad_far = (weight_far * (prob_far - row_dot)).astype(jnp.bfloat16)
    query_sum = jnp.einsum(
        "dbhqk,dbkhe->dbqhe", grad_near, near_k, preferred_element_type=jnp.float32
    )
    query_sum = query_sum + jnp.einsum(
        "dbhqk,dkhe->dbqhe", grad_far, far_k, preferred_element_type=jnp.float32
    )
    query_grad = (
        (query_sum * score_scale).reshape(doc_count, tok_count, head_cols).astype(jnp.bfloat16)
    )
    near_key_rows = (
        jnp.einsum("dbhqk,dbqhe->dbkhe", grad_near, query_heads, preferred_element_type=jnp.float32)
        * score_scale
    )
    near_value_rows = jnp.einsum(
        "dbhqk,dbqhe->dbkhe", rounded_near, grad_heads, preferred_element_type=jnp.float32
    )
    far_key_rows = (
        jnp.einsum("dbhqk,dbqhe->dkhe", grad_far, query_heads, preferred_element_type=jnp.float32)
        * score_scale
    )
    far_value_rows = jnp.einsum(
        "dbhqk,dbqhe->dkhe", rounded_far, grad_heads, preferred_element_type=jnp.float32
    )
    near_rows = jnp.stack([near_key_rows, near_value_rows]).reshape(
        2, doc_count, 2, NEAR + 1, block, head_cols
    )
    back_six = jax.vmap(place_blocks, in_axes=(1, 0), out_axes=1)(near_rows, chosen)
    rims = jnp.concatenate([back_six[:, :, 0:2], back_six[:, :, 4:6]], axis=2).reshape(
        2, doc_count, 2 * tok_count, head_cols
    )
    beside_all = extended(rims, (("seq", 2),), tok_count)
    token_grad = back_six[:, :, 2:4].reshape(2, doc_count, tok_count, head_cols)
    token_grad = token_grad + beside_all[:, :, :tok_count] + beside_all[:, :, 3 * tok_count :]
    far_rows = jnp.stack([far_key_rows, far_value_rows]).reshape(
        2, doc_count, levels, block, head_cols
    )
    carried = jnp.zeros((2, doc_count, block, head_cols), jnp.float32)
    for level_no in reversed(range(levels)):
        message = far_rows[:, :, level_no]
        mine = jnp.zeros_like(message)
        if level_no + 1 < levels:
            upper = position >> level_no & 1 == 1
            spread = jnp.repeat(carried, 2, axis=2) * 0.5
            lower_half = spread[:, :, :block]
            upper_half = spread[:, :, block:]
            mine = jnp.where(upper, upper_half, lower_half)
            message = message + jnp.where(upper, lower_half, upper_half)
        returned = swapped(message, "seq", level_no)
        carried = returned + mine
    token_grad = token_grad + jnp.repeat(carried, 2, axis=2) * 0.5
    key_grad = token_grad[0].astype(jnp.bfloat16)
    value_grad = token_grad[1].astype(jnp.bfloat16)
    return (attention, query_grad, key_grad, value_grad, weight_grad)


def solution(mesh):
    in_specs = (
        P(("groups", "dp"), "seq", "head"),
        P(("groups", "dp"), "seq", "head"),
        P(("groups", "dp"), "seq", "head"),
        P(("groups", "dp"), "seq", None),
        P("seq", "head"),
        P(("groups", "dp"), "seq", None),
    )
    out_specs = (
        P(("groups", "dp"), "seq", "head"),
        P(("groups", "dp"), "seq", "head"),
        P(("groups", "dp"), "seq", "head"),
        P(("groups", "dp"), "seq", "head"),
        P(("groups", "seq"), "head"),
    )
    return jax.shard_map(shards, mesh=mesh, in_specs=in_specs, out_specs=out_specs, check_vma=False)
```

profile of v0, /device:TPU:0, one launch (start us, length us, event | category | flops | bytes accessed | tf_op | source)
XLA Modules:
  0.0 361.2 jit_solution(15132520901967970496)
XLA Ops:
  10.5 6.3 %collective-permute-start = (bf16[2,1,128,1024]{3,2,1,0:T(8,128)(2,1)}, bf16[2,1,128,1024]{3,2,1,0:T(8,128)(2,1)}, u32[]{:S(2)}, u32[]{:S(2)}) collective-permute-start(bf16[2,1,128,1024]{3,2,1,0:T(8,128)(2,1)} %pad_maximum_fusion.4), channel_id=1, source_target_pairs={{0,4},{4,8},{8,12},{1,5},{5,9},{9,13},{2,6},{6,10},{10,14},{3,7},{... | collective-permute-start | bytes 1572872 | tf_op jit(solution)/shard_map/ppermute | solution.py:19
  20.9 2.8 copy.237
  24.2 23.4 %reduce.20 = bf16[4096,128]{1,0:T(8,128)(2,1)} reduce(bf16[4096,1,128]{2,1,0:T(2,128)(2,1)S(1)} %bitcast.213, bf16[]{:T(256)} %broadcast.178), dimensions={1}, to_apply=%bitcast.190.reduce_sub_computation | reduce | bytes 2097154
  47.5 3.5 reshape.524
  51.1 4.7 %all-to-all-start = ((bf16[4,2,65536]{2,1,0:T(2,128)(2,1)}), bf16[4,2,65536]{2,1,0:T(2,128)(2,1)}, u32[]{:S(2)}, u32[]{:S(2)}) async-start(bf16[4,2,65536]{2,1,0:T(2,128)(2,1)} %reshape.524), calls=%async_computation | async-start | bytes 2097152 | tf_op jit(solution)/shard_map/all_to_all | solution.py:114
  58.2 1.8 gather_fusion
  63.0 23.5 %collective-permute-done.2 = f32[2,1,64,1024]{3,2,1,0:T(8,128)} collective-permute-done((f32[2,1,64,1024]{3,2,1,0:T(8,128)}, f32[2,1,64,1024]{3,2,1,0:T(8,128)}, u32[]{:S(2)}, u32[]{:S(2)}) %collective-permute-start.2) | collective-permute-done | bytes 524320 | tf_op jit(solution)/shard_map/ppermute | solution.py:29
  91.6 9.4 %collective-permute-start.3 = (bf16[2,1,64,1024]{3,2,1,0:T(8,128)(2,1)S(1)}, bf16[2,1,64,1024]{3,2,1,0:T(8,128)(2,1)S(1)}, u32[]{:S(2)}, u32[]{:S(2)}) collective-permute-start(bf16[2,1,64,1024]{3,2,1,0:T(8,128)(2,1)S(1)} %fusion.23), channel_id=1, source_target_pairs={{0,8},{4,12},{8,0},{12,4},{1,9},{5,13},{9,1},{13,5},{2,10},{6,14},... | collective-permute-start | bytes 786440 | tf_op jit(solution)/shard_map/ppermute | solution.py:29
  102.8 35.3 %collective-permute-done.3 = bf16[2,1,64,1024]{3,2,1,0:T(8,128)(2,1)S(1)} collective-permute-done((bf16[2,1,64,1024]{3,2,1,0:T(8,128)(2,1)S(1)}, bf16[2,1,64,1024]{3,2,1,0:T(8,128)(2,1)S(1)}, u32[]{:S(2)}, u32[]{:S(2)}) %collective-permute-start.3) | collective-permute-done | bytes 262176 | tf_op jit(solution)/shard_map/ppermute | solution.py:29
  142.3 2.4 convolution_bitcast_fusion.3
  144.7 52.0 %all-gather.3.cloned.1.call-done = bf16[4096,1024]{1,0:T(8,128)(2,1)} async-done(((bf16[1024,1024]{1,0:T(8,128)(2,1)}), bf16[4096,1024]{1,0:T(8,128)(2,1)}) %all-gather.3.cloned.1.call-update) | async-done | bytes 8388624 | tf_op jit(solution)/shard_map/all_gather | solution.py:110
  196.6 4.7 %fusion.8 = bf16[16,8,8,128]{3,1,2,0:T(8,128)(2,1)S(1)} fusion(bf16[4096,1024]{1,0:T(8,128)(2,1)} %all-gather.3.cloned.1.call-done, bf16[1,128,4096]{2,1,0:T(8,128)(2,1)S(1)} %copy-done), kind=kOutput, calls=%fused_computation.24 | convolution fusion | flops 1073872896 | bytes 9699328 | tf_op jit(solution)/shard_map/dot_general | solution.py:111
  206.7 2.6 reshape.525
  212.7 24.6 %all-gather.5.cloned.1.call-done = bf16[1,512,1024]{2,1,0:T(8,128)(2,1)} async-done(((bf16[1,128,1024]{2,1,0:T(8,128)(2,1)}), bf16[1,512,1024]{2,1,0:T(8,128)(2,1)}) %all-gather.5.cloned.1.call-update) | async-done | bytes 1048592 | tf_op jit(solution)/shard_map/all_gather | solution.py:115
  237.3 4.5 %convolution_bitcast_fusion = f32[1024,1024]{0,1:T(8,128)} fusion(bf16[512,1024]{1,0:T(8,128)(2,1)S(1)} %bitcast.233, bf16[1,512,1024]{2,1,0:T(8,128)(2,1)} %all-gather.5.cloned.1.call-done), kind=kOutput, calls=%fused_computation.3 | convolution fusion | flops 1073741824 | bytes 6291456 | tf_op jit(solution)/shard_map/dtc,dtw->cw/dot_general | solution.py:116
  244.6 1.9 collective-permute-start.6
  250.8 3.1 pad_maximum_fusion
  253.9 2.4 copy.255
  256.7 5.4 %scatter_fusion = f32[2,6,64,1024]{3,2,1,0:T(8,128)S(1)} fusion(f32[2,6,64,1024]{3,2,1,0:T(8,128)S(1)} %broadcast.159, s32[6]{0:T(128)S(1)} %reshape.496, f32[6,2,64,1024]{3,2,1,0:T(8,128)} %bitcast.208), kind=kCustom, calls=%fused_computation.1 | custom fusion | flops 786432 | bytes 9437208 | tf_op jit(solution)/shard_map/vmap()/scatter-add | solution.py:45
  266.5 5.5 %collective-permute-start.4 = (f32[2,1,128,1024]{3,2,1,0:T(8,128)}, f32[2,1,128,1024]{3,2,1,0:T(8,128)}, u32[]{:S(2)}, u32[]{:S(2)}) collective-permute-start(f32[2,1,128,1024]{3,2,1,0:T(8,128)} %get-tuple-element.40), channel_id=1, source_target_pairs={{0,4},{4,8},{8,12},{1,5},{5,9},{9,13},{2,6},{6,10},{10,14},{3,7},{... | collective-permute-start | bytes 3145736 | tf_op jit(solution)/shard_map/ppermute | solution.py:19
  276.4 28.1 %collective-permute-done.7 = f32[2,1,64,1024]{3,0,2,1:T(2,128)S(1)} collective-permute-done((f32[2,1,64,1024]{3,0,2,1:T(2,128)S(1)}, f32[2,1,64,1024]{3,0,2,1:T(2,128)S(1)}, u32[]{:S(2)}, u32[]{:S(2)}) %collective-permute-start.7) | collective-permute-done | bytes 524320 | tf_op jit(solution)/shard_map/ppermute | solution.py:29
  306.4 1.9 add_convert_fusion
  309.1 40.2 %all-reduce.2.cloned.1.call-done = f32[1024,1024]{0,1:T(8,128)} async-done(((f32[1024,1024]{0,1:T(8,128)}), f32[1024,1024]{0,1:T(8,128)}) %all-reduce.2.cloned.1.call-update) | async-done | bytes 4194320 | tf_op jit(solution)/shard_map/psum | solution.py:119
  349.4 5.3 %copy.239 = f32[1024,1024]{1,0:T(8,128)} copy(f32[1024,1024]{0,1:T(8,128)} %all-reduce.2.cloned.1.call-done) | data formatting | bytes 8388608
  (152 shorter events, 51.4 us)
Async XLA Ops:
  7.2 189.4 %all-gather.3.cloned.1.call-start = ((), (), s32[]{:S(2)}) async-start(), calls=%async_computation.1 | async-start | bytes 10485760 | tf_op jit(solution)/shard_map/all_gather | solution.py:110
  9.0 11.8 %copy-start = (bf16[1,128,4096]{2,1,0:T(8,128)(2,1)S(1)}, bf16[1,128,4096]{2,1,0:T(8,128)(2,1)}, u32[]{:S(2)}) copy-start(bf16[1,128,4096]{2,1,0:T(8,128)(2,1)} %param.11) | copy-start | bytes 3145732
  9.0 47.8 %collective-permute-start.1 = (bf16[2,1,128,1024]{3,2,1,0:T(8,128)(2,1)}, bf16[2,1,128,1024]{3,2,1,0:T(8,128)(2,1)}, u32[]{:S(2)}, u32[]{:S(2)}) collective-permute-start(bf16[2,1,128,1024]{3,2,1,0:T(8,128)(2,1)} %pad_maximum_fusion.4), channel_id=1, source_target_pairs={{4,0},{8,4},{12,8},{5,1},{9,5},{13,9},{6,2},{10,6},{14,10},{7,3},{... | collective-permute-start | bytes 1572872 | tf_op jit(solution)/shard_map/ppermute | solution.py:21
  10.5 46.4 %collective-permute-start = (bf16[2,1,128,1024]{3,2,1,0:T(8,128)(2,1)}, bf16[2,1,128,1024]{3,2,1,0:T(8,128)(2,1)}, u32[]{:S(2)}, u32[]{:S(2)}) collective-permute-start(bf16[2,1,128,1024]{3,2,1,0:T(8,128)(2,1)} %pad_maximum_fusion.4), channel_id=1, source_target_pairs={{0,4},{4,8},{8,12},{1,5},{5,9},{9,13},{2,6},{6,10},{10,14},{3,7},{... | collective-permute-start | bytes 1572872 | tf_op jit(solution)/shard_map/ppermute | solution.py:19
  19.6 66.9 %collective-permute-start.2 = (f32[2,1,64,1024]{3,2,1,0:T(8,128)}, f32[2,1,64,1024]{3,2,1,0:T(8,128)}, u32[]{:S(2)}, u32[]{:S(2)}) collective-permute-start(f32[2,1,64,1024]{3,2,1,0:T(8,128)} %get-tuple-element.51), channel_id=1, source_target_pairs={{0,4},{4,0},{8,12},{12,8},{1,5},{5,1},{9,13},{13,9},{2,6},{6,2},{1... | collective-permute-start | bytes 1572872 | tf_op jit(solution)/shard_map/ppermute | solution.py:29
  47.5 8.2 %copy-start.29 = (s32[1,2,2]{2,1,0:T(2,128)S(1)}, s32[1,2,2]{2,1,0:T(2,128)}, u32[]{:S(2)}) copy-start(s32[1,2,2]{2,1,0:T(2,128)} %param.9) | copy-start | bytes 52
  47.5 8.4 %copy-start.28 = (bf16[1,128,1024]{2,1,0:T(8,128)(2,1)S(1)}, bf16[1,128,1024]{2,1,0:T(8,128)(2,1)}, u32[]{:S(2)}) copy-start(bf16[1,128,1024]{2,1,0:T(8,128)(2,1)} %param.6) | copy-start | bytes 786436
  51.1 5.8 %copy-start.15 = (bf16[1,128,1024]{2,1,0:T(8,128)(2,1)S(1)}, bf16[1,128,1024]{2,1,0:T(8,128)(2,1)}, u32[]{:S(2)}) copy-start(bf16[1,128,1024]{2,1,0:T(8,128)(2,1)} %param.8) | copy-start | bytes 786436
  51.1 5.8 %copy-start.17 = (bf16[1,128,1024]{2,1,0:T(8,128)(2,1)S(1)}, bf16[1,128,1024]{2,1,0:T(8,128)(2,1)}, u32[]{:S(2)}) copy-start(bf16[1,128,1024]{2,1,0:T(8,128)(2,1)} %param.7) | copy-start | bytes 786436
  51.1 155.7 %all-to-all-start = ((bf16[4,2,65536]{2,1,0:T(2,128)(2,1)}), bf16[4,2,65536]{2,1,0:T(2,128)(2,1)}, u32[]{:S(2)}, u32[]{:S(2)}) async-start(bf16[4,2,65536]{2,1,0:T(2,128)(2,1)} %reshape.524), calls=%async_computation | async-start | bytes 2097152 | tf_op jit(solution)/shard_map/all_to_all | solution.py:114
  55.8 181.5 %all-gather.5.cloned.1.call-start = ((), (), s32[]{:S(2)}) async-start(), calls=%async_computation.2 | async-start | bytes 1310720 | tf_op jit(solution)/shard_map/all_gather | solution.py:115
  61.8 24.7 %copy-start.23 = (f32[2,1,64,1024]{3,2,0,1:T(8,128)S(1)}, f32[2,1,64,1024]{3,2,0,1:T(8,128)}, u32[]{:S(2)}) copy-start(f32[2,1,64,1024]{3,2,0,1:T(8,128)} %get-tuple-element.50) | copy-start | bytes 1572868
  63.0 39.1 %copy-start.1 = (bf16[48,8,8,128]{3,2,1,0:T(8,128)(2,1)}, bf16[48,8,8,128]{3,2,1,0:T(8,128)(2,1)S(1)}, u32[]{:S(2)}) copy-start(bf16[48,8,8,128]{3,2,1,0:T(8,128)(2,1)S(1)} %copy.256) | copy-start | bytes 2359300
  91.6 46.5 %collective-permute-start.3 = (bf16[2,1,64,1024]{3,2,1,0:T(8,128)(2,1)S(1)}, bf16[2,1,64,1024]{3,2,1,0:T(8,128)(2,1)S(1)}, u32[]{:S(2)}, u32[]{:S(2)}) collective-permute-start(bf16[2,1,64,1024]{3,2,1,0:T(8,128)(2,1)S(1)} %fusion.23), channel_id=1, source_target_pairs={{0,8},{4,12},{8,0},{12,4},{1,9},{5,13},{9,1},{13,5},{2,10},{6,14},... | collective-permute-start | bytes 786440 | tf_op jit(solution)/shard_map/ppermute | solution.py:29
  139.0 5.6 %copy-start.18 = (bf16[1,1,128,1024]{2,3,1,0:T(8,128)(2,1)}, bf16[1,1,128,1024]{2,3,1,0:T(8,128)(2,1)S(1)}, u32[]{:S(2)}) copy-start(bf16[1,1,128,1024]{2,3,1,0:T(8,128)(2,1)S(1)} %copy.202) | copy-start | bytes 786436
  196.6 4.8 %copy-start.26 = (bf16[48,8,8,128]{3,2,1,0:T(8,128)(2,1)S(1)}, bf16[48,8,8,128]{3,2,1,0:T(8,128)(2,1)}, u32[]{:S(2)}) copy-start(bf16[48,8,8,128]{3,2,1,0:T(8,128)(2,1)} %copy.258) | copy-start | bytes 2359300
  206.4 143.0 %all-reduce.2.cloned.1.call-start = ((), (), s32[]{:S(2)}) async-start(), calls=%async_computation.3 | async-start | bytes 8388608 | tf_op jit(solution)/shard_map/psum | solution.py:119
  212.6 30.7 %copy-start.5 = (f32[1,128,8,128]{3,2,0,1:T(8,128)}, f32[1,128,8,128]{3,2,0,1:T(8,128)S(1)}, u32[]{:S(2)}) copy-start(f32[1,128,8,128]{3,2,0,1:T(8,128)S(1)} %copy.233) | copy-start | bytes 1572868
  244.6 27.4 %collective-permute-start.6 = (f32[2,1,64,1024]{3,0,2,1:T(2,128)}, f32[2,1,64,1024]{3,0,2,1:T(2,128)}, u32[]{:S(2)}, u32[]{:S(2)}) collective-permute-start(f32[2,1,64,1024]{3,0,2,1:T(2,128)} %fusion.21), channel_id=1, source_target_pairs={{0,8},{4,12},{8,0},{12,4},{1,9},{5,13},{9,1},{13,5},{2,10},{6,14},... | collective-permute-start | bytes 1572872 | tf_op jit(solution)/shard_map/ppermute | solution.py:29
  265.1 8.6 %copy-start.6 = (f32[1,128,8,128]{3,2,0,1:T(8,128)S(1)}, f32[1,128,8,128]{3,2,0,1:T(8,128)}, u32[]{:S(2)}) copy-start(f32[1,128,8,128]{3,2,0,1:T(8,128)} %copy-done.5) | copy-start | bytes 1572868
  265.1 8.6 %copy-start.8 = (f32[1,128,8,128]{3,2,0,1:T(8,128)S(1)}, f32[1,128,8,128]{3,2,0,1:T(8,128)}, u32[]{:S(2)}) copy-start(f32[1,128,8,128]{3,2,0,1:T(8,128)} %copy-done.7) | copy-start | bytes 1572868
  265.1 41.2 %collective-permute-start.5 = (f32[2,1,128,1024]{3,2,1,0:T(8,128)}, f32[2,1,128,1024]{3,2,1,0:T(8,128)}, u32[]{:S(2)}, u32[]{:S(2)}) collective-permute-start(f32[2,1,128,1024]{3,2,1,0:T(8,128)} %get-tuple-element.41), channel_id=1, source_target_pairs={{4,0},{8,4},{12,8},{5,1},{9,5},{13,9},{6,2},{10,6},{14,10},{7,3},{... | collective-permute-start | bytes 3145736 | tf_op jit(solution)/shard_map/ppermute | solution.py:21
  266.5 39.8 %collective-permute-start.4 = (f32[2,1,128,1024]{3,2,1,0:T(8,128)}, f32[2,1,128,1024]{3,2,1,0:T(8,128)}, u32[]{:S(2)}, u32[]{:S(2)}) collective-permute-start(f32[2,1,128,1024]{3,2,1,0:T(8,128)} %get-tuple-element.40), channel_id=1, source_target_pairs={{0,4},{4,8},{8,12},{1,5},{5,9},{9,13},{2,6},{6,10},{10,14},{3,7},{... | collective-permute-start | bytes 3145736 | tf_op jit(solution)/shard_map/ppermute | solution.py:19
  274.5 30.0 %collective-permute-start.7 = (f32[2,1,64,1024]{3,0,2,1:T(2,128)S(1)}, f32[2,1,64,1024]{3,0,2,1:T(2,128)S(1)}, u32[]{:S(2)}, u32[]{:S(2)}) collective-permute-start(f32[2,1,64,1024]{3,0,2,1:T(2,128)S(1)} %fusion.20), channel_id=1, source_target_pairs={{0,4},{4,0},{8,12},{12,8},{1,5},{5,1},{9,13},{13,9},{2,6},{6,2},{1... | collective-permute-start | bytes 1572872 | tf_op jit(solution)/shard_map/ppermute | solution.py:29
  (18 other events, 26.4 us)
Sparse Core Ops, SparseCore 0:
  9.6 186.9 all-gather.2
  206.5 30.7 all-gather.4
  242.0 107.3 all-reduce.1
where the time goes:
time: 362 us; the launch traced here: 361 us
  waiting for transfers between devices  204 us (56%)
  other arithmetic  51.9 us (14%)
  local copies, waits for them, and re-layouts  39.6 us (11%)
  starting transfers between devices  32.3 us (9%)
  matrix products  18.6 us (5%)
  between operations  14.4 us (4%)
    ppermute x4, waiting for transfers between devices, swapped(): lax.ppermute(shard, axis, [(i, i ^ 1 << stride) for i in range(lax.axis_s...  86.9 us
    all_gather x1, waiting for transfers between devices, shards(): whole_weight = lax.all_gather(out_weight, 'seq', axis=0, tiled=True)  52 us
    psum x1, waiting for transfers between devices, shards(): weight_grad = lax.psum(weight_part, 'dp')  40.2 us
    all_gather x1, waiting for transfers between devices, shards(): whole_output = lax.all_gather(attention, 'seq', axis=1, tiled=True)  24.6 us
    unnamed x1, other arithmetic  23.4 us
    unnamed x70, local copies, waits for them, and re-layouts  19.1 us
    ppermute x4, starting transfers between devices, swapped(): lax.ppermute(shard, axis, [(i, i ^ 1 << stride) for i in range(lax.axis_s...  12.6 us
    ppermute x2, starting transfers between devices, extended(): lax.ppermute(tail, axis, [(i, (i + 1) % count) for i in range(ends)])  11.9 us
  transfers between devices with their start and end apart: 12, of which 6 were waited for; matrix products, arithmetic and copies ran while one was open for 27% of the time, Pallas kernels for 0%

commit v1 on v0

--- a/solution.py
+++ b/solution.py
@@ -116,7 +116,7 @@
     weight_part = jnp.einsum(
         "dtc,dtw->cw", by_feature, whole_output, preferred_element_type=jnp.float32
     )
-    weight_grad = lax.psum(weight_part, "dp")
+    weight_grad = jnp.sum(lax.all_gather(weight_part, "dp"), axis=0)
     grad_heads = attn_grad.reshape(doc_count, 2, block, heads, HEAD_DIM)
     prob_near = jnp.einsum(
         "dbqhe,dbkhe->dbhqk", grad_heads, near_v, preferred_element_type=jnp.float32

time: 362 us -> 389 us (1.075); the launches traced: 361 us -> 382 us
  local copies, waits for them, and re-layouts: 39.6 us -> 55.6 us
  other arithmetic: 51.9 us -> 62.6 us
  waiting for transfers between devices: 204 us -> 196 us
    psum x1 -> x0, waiting for transfers between devices: 40.2 us -> none  [shards(): weight_grad = lax.psum(weight_part, 'dp')]
    all_gather x0 -> x1, waiting for transfers between devices: none -> 33.3 us  [shards(): weight_grad = jnp.sum(lax.all_gather(weight_part, 'dp'), axis=0)]
    reduce_sum x0 -> x1, other arithmetic: none -> 12.9 us  [shards(): weight_grad = jnp.sum(lax.all_gather(weight_part, 'dp'), axis=0)]
    all_gather x0 -> x1, local copies, waits for them, and re-layouts: none -> 11.7 us  [shards(): weight_grad = jnp.sum(lax.all_gather(weight_part, 'dp'), axis=0)]
    unnamed x70 -> x60, local copies, waits for them, and re-layouts: 19.1 us -> 22.2 us
where the time goes in v1:
time: 389 us; the launch traced here: 382 us
  waiting for transfers between devices  196 us (50%)
  other arithmetic  62.6 us (16%)
  local copies, waits for them, and re-layouts  55.6 us (14%)
  starting transfers between devices  32.7 us (8%)
  matrix products  19.9 us (5%)
  between operations  14.6 us (4%)
    ppermute x4, waiting for transfers between devices, swapped(): lax.ppermute(shard, axis, [(i, i ^ 1 << stride) for i in range(lax.axis_s...  86.3 us
    all_gather x1, waiting for transfers between devices, shards(): whole_weight = lax.all_gather(out_weight, 'seq', axis=0, tiled=True)  52.6 us
    all_gather x1, waiting for transfers between devices, shards(): weight_grad = jnp.sum(lax.all_gather(weight_part, 'dp'), axis=0)  33.3 us
    all_gather x1, waiting for transfers between devices, shards(): whole_output = lax.all_gather(attention, 'seq', axis=1, tiled=True)  23.6 us
    unnamed x1, other arithmetic  23.4 us
    unnamed x60, local copies, waits for them, and re-layouts  22.2 us
    reduce_sum x1, other arithmetic, shards(): weight_grad = jnp.sum(lax.all_gather(weight_part, 'dp'), axis=0)  12.9 us
    ppermute x4, starting transfers between devices, swapped(): lax.ppermute(shard, axis, [(i, i ^ 1 << stride) for i in range(lax.axis_s...  12.5 us
  transfers between devices with their start and end apart: 12, of which 6 were waited for; matrix products, arithmetic and copies ran while one was open for 27% of the time, Pallas kernels for 0%

profile of v1, /device:TPU:0, one launch (start us, length us, event | category | flops | bytes accessed | tf_op | source)
XLA Modules:
  0.0 381.9 jit_solution(4300320895631346416)
XLA Ops:
  10.5 6.4 %collective-permute-start = (bf16[2,1,128,1024]{3,2,1,0:T(8,128)(2,1)}, bf16[2,1,128,1024]{3,2,1,0:T(8,128)(2,1)}, u32[]{:S(2)}, u32[]{:S(2)}) collective-permute-start(bf16[2,1,128,1024]{3,2,1,0:T(8,128)(2,1)} %pad_maximum_fusion.4), channel_id=1, source_target_pairs={{0,4},{4,8},{8,12},{1,5},{5,9},{9,13},{2,6},{6,10},{10,14},{3,7},{... | collective-permute-start | bytes 1572872 | tf_op jit(solution)/shard_map/ppermute | solution.py:19
  20.9 2.8 copy.234
  24.2 23.4 %reduce.20 = bf16[4096,128]{1,0:T(8,128)(2,1)} reduce(bf16[4096,1,128]{2,1,0:T(2,128)(2,1)S(1)} %bitcast.215, bf16[]{:T(256)} %broadcast.178), dimensions={1}, to_apply=%bitcast.192.reduce_sub_computation | reduce | bytes 2097154
  47.6 3.5 reshape.525
  51.1 4.7 %all-to-all-start = ((bf16[4,2,65536]{2,1,0:T(2,128)(2,1)}), bf16[4,2,65536]{2,1,0:T(2,128)(2,1)}, u32[]{:S(2)}, u32[]{:S(2)}) async-start(bf16[4,2,65536]{2,1,0:T(2,128)(2,1)} %reshape.525), calls=%async_computation | async-start | bytes 2097152 | tf_op jit(solution)/shard_map/all_to_all | solution.py:114
  64.4 22.1 %collective-permute-done.2 = f32[2,1,64,1024]{3,2,1,0:T(8,128)} collective-permute-done((f32[2,1,64,1024]{3,2,1,0:T(8,128)}, f32[2,1,64,1024]{3,2,1,0:T(8,128)}, u32[]{:S(2)}, u32[]{:S(2)}) %collective-permute-start.2) | collective-permute-done | bytes 524320 | tf_op jit(solution)/shard_map/ppermute | solution.py:29
  89.9 9.3 %collective-permute-start.3 = (bf16[2,1,64,1024]{3,2,1,0:T(8,128)(2,1)S(1)}, bf16[2,1,64,1024]{3,2,1,0:T(8,128)(2,1)S(1)}, u32[]{:S(2)}, u32[]{:S(2)}) collective-permute-start(bf16[2,1,64,1024]{3,2,1,0:T(8,128)(2,1)S(1)} %fusion.23), channel_id=1, source_target_pairs={{0,8},{4,12},{8,0},{12,4},{1,9},{5,13},{9,1},{13,5},{2,10},{6,14},... | collective-permute-start | bytes 786440 | tf_op jit(solution)/shard_map/ppermute | solution.py:29
  102.1 36.1 %collective-permute-done.3 = bf16[2,1,64,1024]{3,2,1,0:T(8,128)(2,1)S(1)} collective-permute-done((bf16[2,1,64,1024]{3,2,1,0:T(8,128)(2,1)S(1)}, bf16[2,1,64,1024]{3,2,1,0:T(8,128)(2,1)S(1)}, u32[]{:S(2)}, u32[]{:S(2)}) %collective-permute-start.3) | collective-permute-done | bytes 262176 | tf_op jit(solution)/shard_map/ppermute | solution.py:29
  141.6 2.4 convolution_bitcast_fusion.3
  144.0 52.6 %all-gather.5.cloned.1.call-done = bf16[4096,1024]{1,0:T(8,128)(2,1)} async-done(((bf16[1024,1024]{1,0:T(8,128)(2,1)}), bf16[4096,1024]{1,0:T(8,128)(2,1)}) %all-gather.5.cloned.1.call-update) | async-done | bytes 8388624 | tf_op jit(solution)/shard_map/all_gather | solution.py:110
  196.7 4.7 %fusion.8 = bf16[16,8,8,128]{3,1,2,0:T(8,128)(2,1)S(1)} fusion(bf16[4096,1024]{1,0:T(8,128)(2,1)} %all-gather.5.cloned.1.call-done, bf16[1,128,4096]{2,1,0:T(8,128)(2,1)S(1)} %copy-done), kind=kOutput, calls=%fused_computation.24 | convolution fusion | flops 1073872896 | bytes 9699328 | tf_op jit(solution)/shard_map/dot_general | solution.py:111
  206.1 4.0 %reshape.526 = bf16[4096,1,128]{2,1,0:T(2,128)(2,1)} reshape(bf16[4,2,65536]{2,1,0:T(2,128)(2,1)} %all-to-all-done) | data formatting | bytes 2097152
  213.1 23.6 %all-gather.7.cloned.1.call-done = bf16[1,512,1024]{2,1,0:T(8,128)(2,1)} async-done(((bf16[1,128,1024]{2,1,0:T(8,128)(2,1)}), bf16[1,512,1024]{2,1,0:T(8,128)(2,1)}) %all-gather.7.cloned.1.call-update) | async-done | bytes 1048592 | tf_op jit(solution)/shard_map/all_gather | solution.py:115
  236.7 4.8 %convolution_bitcast_fusion = f32[1024,1024]{0,1:T(8,128)} fusion(bf16[512,1024]{1,0:T(8,128)(2,1)} %bitcast.235, bf16[1,512,1024]{2,1,0:T(8,128)(2,1)} %all-gather.7.cloned.1.call-done), kind=kOutput, calls=%fused_computation.3 | convolution fusion | flops 1073741824 | bytes 6291456 | tf_op jit(solution)/shard_map/dtc,dtw->cw/dot_general | solution.py:116
  246.1 1.9 collective-permute-start.6
  253.3 3.1 pad_maximum_fusion
  256.4 2.4 copy.252
  259.2 5.7 %scatter_fusion = f32[2,6,64,1024]{3,2,1,0:T(8,128)S(1)} fusion(f32[2,6,64,1024]{3,2,1,0:T(8,128)S(1)} %broadcast.159, s32[6]{0:T(128)S(1)} %reshape.496, f32[6,2,64,1024]{3,2,1,0:T(8,128)} %bitcast.210), kind=kCustom, calls=%fused_computation.1 | custom fusion | flops 786432 | bytes 9437208 | tf_op jit(solution)/shard_map/vmap()/scatter-add | solution.py:45
  269.5 5.5 %collective-permute-start.4 = (f32[2,1,128,1024]{3,2,1,0:T(8,128)}, f32[2,1,128,1024]{3,2,1,0:T(8,128)}, u32[]{:S(2)}, u32[]{:S(2)}) collective-permute-start(f32[2,1,128,1024]{3,2,1,0:T(8,128)} %get-tuple-element.25), channel_id=1, source_target_pairs={{0,4},{4,8},{8,12},{1,5},{5,9},{9,13},{2,6},{6,10},{10,14},{3,7},{... | collective-permute-start | bytes 3145736 | tf_op jit(solution)/shard_map/ppermute | solution.py:19
  279.3 28.0 %collective-permute-done.7 = f32[2,1,64,1024]{3,0,2,1:T(2,128)S(1)} collective-permute-done((f32[2,1,64,1024]{3,0,2,1:T(2,128)S(1)}, f32[2,1,64,1024]{3,0,2,1:T(2,128)S(1)}, u32[]{:S(2)}, u32[]{:S(2)}) %collective-permute-start.7) | collective-permute-done | bytes 524320 | tf_op jit(solution)/shard_map/ppermute | solution.py:29
  311.9 33.3 %all-gather.9.cloned.1.call-done = f32[2048,1024]{0,1:T(8,128)} async-done(((f32[1024,1024]{0,1:T(8,128)}), f32[2048,1024]{0,1:T(8,128)}) %all-gather.9.cloned.1.call-update) | async-done | bytes 8388624 | tf_op jit(solution)/shard_map/all_gather | solution.py:119
  345.2 11.7 %reshape.502 = f32[2,1024,1024]{1,0,2:T(2,128)} reshape(f32[2048,1024]{0,1:T(8,128)} %all-gather.9.cloned.1.call-done) | data formatting | bytes 16777216 | tf_op jit(solution)/shard_map/all_gather | solution.py:119
  356.9 12.9 %reduce_sum.69 = f32[1024,1024]{0,1:T(8,128)} reduce(f32[2,1024,1024]{1,0,2:T(2,128)} %reshape.502, f32[]{:T(128)} %constant.15.clone.1), dimensions={0}, to_apply=%region_9.10 | reduce | flops 1048576 | bytes 12582916 | tf_op jit(solution)/shard_map/reduce_sum | solution.py:119
  369.8 5.3 %copy.236 = f32[1024,1024]{1,0:T(8,128)} copy(f32[1024,1024]{0,1:T(8,128)} %reduce_sum.69) | data formatting | bytes 8388608
  (144 shorter events, 56.9 us)
Async XLA Ops:
  7.2 189.5 %all-gather.5.cloned.1.call-start = ((), (), s32[]{:S(2)}) async-start(), calls=%async_computation.1 | async-start | bytes 10485760 | tf_op jit(solution)/shard_map/all_gather | solution.py:110
  9.0 11.9 %copy-start = (bf16[1,128,4096]{2,1,0:T(8,128)(2,1)S(1)}, bf16[1,128,4096]{2,1,0:T(8,128)(2,1)}, u32[]{:S(2)}) copy-start(bf16[1,128,4096]{2,1,0:T(8,128)(2,1)} %param.11) | copy-start | bytes 3145732
  9.0 48.3 %collective-permute-start.1 = (bf16[2,1,128,1024]{3,2,1,0:T(8,128)(2,1)}, bf16[2,1,128,1024]{3,2,1,0:T(8,128)(2,1)}, u32[]{:S(2)}, u32[]{:S(2)}) collective-permute-start(bf16[2,1,128,1024]{3,2,1,0:T(8,128)(2,1)} %pad_maximum_fusion.4), channel_id=1, source_target_pairs={{4,0},{8,4},{12,8},{5,1},{9,5},{13,9},{6,2},{10,6},{14,10},{7,3},{... | collective-permute-start | bytes 1572872 | tf_op jit(solution)/shard_map/ppermute | solution.py:21
  10.5 46.9 %collective-permute-start = (bf16[2,1,128,1024]{3,2,1,0:T(8,128)(2,1)}, bf16[2,1,128,1024]{3,2,1,0:T(8,128)(2,1)}, u32[]{:S(2)}, u32[]{:S(2)}) collective-permute-start(bf16[2,1,128,1024]{3,2,1,0:T(8,128)(2,1)} %pad_maximum_fusion.4), channel_id=1, source_target_pairs={{0,4},{4,8},{8,12},{1,5},{5,9},{9,13},{2,6},{6,10},{10,14},{3,7},{... | collective-permute-start | bytes 1572872 | tf_op jit(solution)/shard_map/ppermute | solution.py:19
  19.7 66.9 %collective-permute-start.2 = (f32[2,1,64,1024]{3,2,1,0:T(8,128)}, f32[2,1,64,1024]{3,2,1,0:T(8,128)}, u32[]{:S(2)}, u32[]{:S(2)}) collective-permute-start(f32[2,1,64,1024]{3,2,1,0:T(8,128)} %get-tuple-element.36), channel_id=1, source_target_pairs={{0,4},{4,0},{8,12},{12,8},{1,5},{5,1},{9,13},{13,9},{2,6},{6,2},{1... | collective-permute-start | bytes 1572872 | tf_op jit(solution)/shard_map/ppermute | solution.py:29
  47.6 8.7 %copy-start.24 = (s32[1,2,2]{2,1,0:T(2,128)S(1)}, s32[1,2,2]{2,1,0:T(2,128)}, u32[]{:S(2)}) copy-start(s32[1,2,2]{2,1,0:T(2,128)} %param.9) | copy-start | bytes 52
  47.6 8.9 %copy-start.23 = (bf16[1,128,1024]{2,1,0:T(8,128)(2,1)S(1)}, bf16[1,128,1024]{2,1,0:T(8,128)(2,1)}, u32[]{:S(2)}) copy-start(bf16[1,128,1024]{2,1,0:T(8,128)(2,1)} %param.6) | copy-start | bytes 786436
  51.1 6.2 %copy-start.11 = (bf16[1,128,1024]{2,1,0:T(8,128)(2,1)S(1)}, bf16[1,128,1024]{2,1,0:T(8,128)(2,1)}, u32[]{:S(2)}) copy-start(bf16[1,128,1024]{2,1,0:T(8,128)(2,1)} %param.7) | copy-start | bytes 786436
  51.1 154.9 %all-to-all-start = ((bf16[4,2,65536]{2,1,0:T(2,128)(2,1)}), bf16[4,2,65536]{2,1,0:T(2,128)(2,1)}, u32[]{:S(2)}, u32[]{:S(2)}) async-start(bf16[4,2,65536]{2,1,0:T(2,128)(2,1)} %reshape.525), calls=%async_computation | async-start | bytes 2097152 | tf_op jit(solution)/shard_map/all_to_all | solution.py:114
  55.8 180.9 %all-gather.7.cloned.1.call-start = ((), (), s32[]{:S(2)}) async-start(), calls=%async_computation.2 | async-start | bytes 1310720 | tf_op jit(solution)/shard_map/all_gather | solution.py:115
  62.3 24.3 %copy-start.18 = (f32[2,1,64,1024]{3,2,0,1:T(8,128)S(1)}, f32[2,1,64,1024]{3,2,0,1:T(8,128)}, u32[]{:S(2)}) copy-start(f32[2,1,64,1024]{3,2,0,1:T(8,128)} %get-tuple-element.35) | copy-start | bytes 1572868
  89.8 49.3 %copy-start.20 = (bf16[2,64,8,128]{3,1,0,2:T(8,128)(2,1)S(1)}, bf16[2,64,8,128]{3,1,0,2:T(8,128)(2,1)}, u32[]{:S(2)}) copy-start(bf16[2,64,8,128]{3,1,0,2:T(8,128)(2,1)} %copy.201) | copy-start | bytes 786436
  89.9 48.4 %collective-permute-start.3 = (bf16[2,1,64,1024]{3,2,1,0:T(8,128)(2,1)S(1)}, bf16[2,1,64,1024]{3,2,1,0:T(8,128)(2,1)S(1)}, u32[]{:S(2)}, u32[]{:S(2)}) collective-permute-start(bf16[2,1,64,1024]{3,2,1,0:T(8,128)(2,1)S(1)} %fusion.23), channel_id=1, source_target_pairs={{0,8},{4,12},{8,0},{12,4},{1,9},{5,13},{9,1},{13,5},{2,10},{6,14},... | collective-permute-start | bytes 786440 | tf_op jit(solution)/shard_map/ppermute | solution.py:29
  139.1 4.9 %copy-start.12 = (bf16[1,1,128,1024]{2,3,1,0:T(8,128)(2,1)}, bf16[1,1,128,1024]{2,3,1,0:T(8,128)(2,1)S(1)}, u32[]{:S(2)}) copy-start(bf16[1,1,128,1024]{2,3,1,0:T(8,128)(2,1)S(1)} %copy.199) | copy-start | bytes 786436
  140.7 62.5 %copy-start.14 = (bf16[1,1,128,1024]{2,3,1,0:T(8,128)(2,1)}, bf16[1,1,128,1024]{2,3,1,0:T(8,128)(2,1)S(1)}, u32[]{:S(2)}) copy-start(bf16[1,1,128,1024]{2,3,1,0:T(8,128)(2,1)S(1)} %copy.206) | copy-start | bytes 786436
  196.7 4.8 %copy-start.21 = (bf16[48,8,8,128]{3,2,1,0:T(8,128)(2,1)S(1)}, bf16[48,8,8,128]{3,2,1,0:T(8,128)(2,1)}, u32[]{:S(2)}) copy-start(bf16[48,8,8,128]{3,2,1,0:T(8,128)(2,1)} %copy.255) | copy-start | bytes 2359300
  205.8 139.4 %all-gather.9.cloned.1.call-start = ((), (), s32[]{:S(2)}) async-start(), calls=%async_computation.3 | async-start | bytes 12582912 | tf_op jit(solution)/shard_map/all_gather | solution.py:119
  242.5 6.7 %copy-start.4 = (f32[1,128,8,128]{3,2,0,1:T(8,128)}, f32[1,128,8,128]{3,2,0,1:T(8,128)S(1)}, u32[]{:S(2)}) copy-start(f32[1,128,8,128]{3,2,0,1:T(8,128)S(1)} %copy.230) | copy-start | bytes 1572868
  246.1 28.9 %collective-permute-start.6 = (f32[2,1,64,1024]{3,0,2,1:T(2,128)}, f32[2,1,64,1024]{3,0,2,1:T(2,128)}, u32[]{:S(2)}, u32[]{:S(2)}) collective-permute-start(f32[2,1,64,1024]{3,0,2,1:T(2,128)} %fusion.21), channel_id=1, source_target_pairs={{0,8},{4,12},{8,0},{12,4},{1,9},{5,13},{9,1},{13,5},{2,10},{6,14},... | collective-permute-start | bytes 1572872 | tf_op jit(solution)/shard_map/ppermute | solution.py:29
  268.1 8.6 %copy-start.5 = (f32[1,128,8,128]{3,2,0,1:T(8,128)S(1)}, f32[1,128,8,128]{3,2,0,1:T(8,128)}, u32[]{:S(2)}) copy-start(f32[1,128,8,128]{3,2,0,1:T(8,128)} %copy-done.4) | copy-start | bytes 1572868
  268.1 8.6 %copy-start.7 = (f32[1,128,8,128]{3,2,0,1:T(8,128)S(1)}, f32[1,128,8,128]{3,2,0,1:T(8,128)}, u32[]{:S(2)}) copy-start(f32[1,128,8,128]{3,2,0,1:T(8,128)} %copy-done.6) | copy-start | bytes 1572868
  268.1 41.0 %collective-permute-start.5 = (f32[2,1,128,1024]{3,2,1,0:T(8,128)}, f32[2,1,128,1024]{3,2,1,0:T(8,128)}, u32[]{:S(2)}, u32[]{:S(2)}) collective-permute-start(f32[2,1,128,1024]{3,2,1,0:T(8,128)} %get-tuple-element.26), channel_id=1, source_target_pairs={{4,0},{8,4},{12,8},{5,1},{9,5},{13,9},{6,2},{10,6},{14,10},{7,3},{... | collective-permute-start | bytes 3145736 | tf_op jit(solution)/shard_map/ppermute | solution.py:21
  269.5 39.6 %collective-permute-start.4 = (f32[2,1,128,1024]{3,2,1,0:T(8,128)}, f32[2,1,128,1024]{3,2,1,0:T(8,128)}, u32[]{:S(2)}, u32[]{:S(2)}) collective-permute-start(f32[2,1,128,1024]{3,2,1,0:T(8,128)} %get-tuple-element.25), channel_id=1, source_target_pairs={{0,4},{4,8},{8,12},{1,5},{5,9},{9,13},{2,6},{6,10},{10,14},{3,7},{... | collective-permute-start | bytes 3145736 | tf_op jit(solution)/shard_map/ppermute | solution.py:19
  277.4 29.9 %collective-permute-start.7 = (f32[2,1,64,1024]{3,0,2,1:T(2,128)S(1)}, f32[2,1,64,1024]{3,0,2,1:T(2,128)S(1)}, u32[]{:S(2)}, u32[]{:S(2)}) collective-permute-start(f32[2,1,64,1024]{3,0,2,1:T(2,128)S(1)} %fusion.20), channel_id=1, source_target_pairs={{0,4},{4,0},{8,12},{12,8},{1,5},{5,1},{9,13},{13,9},{2,6},{6,2},{1... | collective-permute-start | bytes 1572872 | tf_op jit(solution)/shard_map/ppermute | solution.py:29
  (13 other events, 18.6 us)
Sparse Core Ops, SparseCore 0:
  9.6 187.0 all-gather.4
  206.0 30.6 all-gather.6
  241.7 103.4 all-gather.8
